TPU v7x, 1024 devices: a whole 4x4x32 slice. The times are simulated.
1024 devices in a mesh: ctx: 64 (over x, y, z_hi, core), fsdp: 16 (over z_lo).
Axes of the slice: x: 4, y: 4, z: 32 (z_hi: 2, z_lo: 16; z = z_hi * 16 + z_lo), core: 2. Of those that a mesh axis runs over, the one named last changes fastest.
Arguments:
- hidden: bfloat16 [2, 16, 4096, 3584], P(None, 'fsdp', 'ctx'), may hold values from -6 to 6
- queries: bfloat16 [2, 16, 4096, 1792], P(None, 'fsdp', 'ctx'), may hold values from -180 to 180
- kv_panel: bfloat16 [2, 3584, 256], P(None, 'fsdp'), may hold values from -0.09375 to 0.09375
- layout: int32 [16, 64], P('fsdp'), may hold values from 0 to 63, each once within a row
Outputs:
- attended: bfloat16 [2, 16, 4096, 1792], P(None, 'fsdp', 'ctx')
Inputs may be any that keep to these rules, and one draw needn't show every extreme that they name: `layout`: each row names every block number of a sequence once.
All inputs are finite; a program needn't handle non-finite values.
Results may differ from a plain program's by a relative error of at most 0.02.
The roundings to bfloat16 on the way count: a program that leaves them out, or rounds other values in their place, can miss the bound.
Values may be sent and summed in bfloat16 or wider, within the bound.
No kernel may reach another device: no remote copies, remote signals or barrier semaphores. Data moves between devices by JAX's collectives and lax.ppermute only.
A program may use at most 32 MiB of HBM per device.

v0:
```python
import math

import jax
import jax.numpy as jnp
from jax import lax
from jax.sharding import PartitionSpec as P

NEGATIVE = -1e30


def rotate_keys(vectors_in, positions, head_dim):
    half_dim = head_dim // 2
    inverse = 1000000.0 ** (-(jnp.arange(half_dim, dtype=jnp.float32) * 2.0 / head_dim))
    angles = positions.astype(jnp.float32)[:, None] * inverse[None, :]
    cosine = jnp.cos(angles)[:, None, :]
    sine_part = jnp.sin(angles)[:, None, :]
    first_half = vectors_in[..., :half_dim]
    second_half = vectors_in[..., half_dim:]
    return jnp.concatenate(
        [
            first_half * cosine - second_half * sine_part,
            second_half * cosine + first_half * sine_part,
        ],
        axis=-1,
    )


def absorb(fold_carry, query_rows, key_part, value_part, allowed, score_scale):
    running, denominator, numerator = fold_carry
    scores = (
        jnp.einsum("tgpd,ugd->gptu", query_rows, key_part, preferred_element_type=jnp.float32)
        * score_scale
    )
    allowed_all = allowed[None, None]
    scores = jnp.where(allowed_all, scores, NEGATIVE)
    highest = jnp.maximum(running, jnp.max(scores, axis=-1))
    factor = jnp.exp(running - highest)
    weights = jnp.where(allowed_all, jnp.exp(scores - highest[..., None]), 0.0)
    denominator = denominator * factor + jnp.sum(weights, axis=-1)
    numerator = numerator * factor[..., None] + jnp.einsum(
        "gptu,ugd->gptd",
        weights.astype(jnp.bfloat16),
        value_part,
        preferred_element_type=jnp.float32,
    )
    return (highest, denominator, numerator)


def absorb_tile(fold_carry, query_rows, key_part, value_part, allowed, score_scale):
    return absorb(fold_carry, query_rows, key_part, value_part, allowed, score_scale)


def absorb_tiled(fold_carry, query_rows, key_part, value_part, allowed, score_scale):
    key_count = key_part.shape[0]
    tile_width = math.gcd(key_count, 512)

    def one_tile(tile_index, inner):
        tile_start = tile_index * tile_width
        return absorb_tile(
            inner,
            query_rows,
            lax.dynamic_slice_in_dim(key_part, tile_start, tile_width, 0),
            lax.dynamic_slice_in_dim(value_part, tile_start, tile_width, 0),
            lax.dynamic_slice_in_dim(allowed, tile_start, tile_width, 1),
            score_scale,
        )

    return lax.fori_loop(0, key_count // tile_width, one_tile, fold_carry)


def clean_mask(block_table, block_limit, block_len):
    key_block = jnp.broadcast_to(block_table[:, None], (block_table.shape[0], block_len)).reshape(
        -1
    )
    return key_block[None, :] < block_limit[:, None]


def start_state(query_rows, noisy_keys, noisy_values, block_len, score_scale):
    heads_here = query_rows.shape[1]
    group_size = query_rows.shape[2]
    head_dim = query_rows.shape[3]
    rows_all = 2 * block_len
    fold_carry = (
        jnp.full((heads_here, group_size, rows_all), NEGATIVE, jnp.float32),
        jnp.zeros((heads_here, group_size, rows_all), jnp.float32),
        jnp.zeros((heads_here, group_size, rows_all, head_dim), jnp.float32),
    )
    allowed = jnp.broadcast_to((jnp.arange(rows_all) >= block_len)[:, None], (rows_all, block_len))
    return absorb(fold_carry, query_rows, noisy_keys, noisy_values, allowed, score_scale)


def finish(fold_carry):
    highest, denominator, numerator = fold_carry
    return jnp.transpose(numerator / denominator[..., None], (2, 0, 1, 3))


def make_panel(token_rows):

    def add_panel(fold_carry, shard_piece, first_row):
        return jnp.einsum(
            "td,hde->the", token_rows, shard_piece, preferred_element_type=jnp.float32
        )

    return add_panel


def local(hidden, queries, kv_panel, layout):
    block_len = hidden.shape[2]
    model_width = hidden.shape[3]
    heads_kv = kv_panel.shape[0]
    head_dim = kv_panel.shape[2] // 2
    group_size = queries.shape[3] // (heads_kv * head_dim)
    score_scale = head_dim ** (-0.5)
    token_rows = hidden.reshape(2 * block_len, model_width)
    query_rows = queries.reshape(2 * block_len, heads_kv, group_size, head_dim)
    block_table = layout[0]
    own_block = lax.dynamic_index_in_dim(block_table, lax.axis_index("ctx"), 0, keepdims=False)
    positions = own_block * block_len + jnp.arange(block_len, dtype=jnp.int32)
    positions = jnp.concatenate([positions, positions])
    block_limit = (
        jnp.concatenate([jnp.ones((block_len,), jnp.int32), jnp.zeros((block_len,), jnp.int32)])
        + own_block
    )
    allowed = clean_mask(block_table, block_limit, block_len)
    add_panel = make_panel(token_rows)
    zero_start = jnp.zeros((2 * block_len, heads_kv, 2 * head_dim), jnp.float32)
    projected = add_panel(
        zero_start, lax.all_gather(kv_panel, "fsdp", axis=1, tiled=True), jnp.int32(0)
    )
    key_rows = rotate_keys(projected[..., :head_dim], positions, head_dim).astype(jnp.bfloat16)
    value_rows = projected[..., head_dim:].astype(jnp.bfloat16)
    key_rows, value_rows = (key_rows, value_rows)
    fold_state = start_state(
        query_rows, key_rows[block_len:], value_rows[block_len:], block_len, score_scale
    )
    clean_keys, clean_values = (
        lax.all_gather(key_rows[:block_len], "ctx", axis=0, tiled=True),
        lax.all_gather(value_rows[:block_len], "ctx", axis=0, tiled=True),
    )
    fold_state = absorb_tiled(
        fold_state, query_rows, clean_keys, clean_values, allowed, score_scale
    )
    attended = finish(fold_state)
    return attended.reshape(2, 1, block_len, heads_kv * group_size * head_dim).astype(jnp.bfloat16)


def solution(mesh):
    return jax.shard_map(
        local,
        mesh=mesh,
        in_specs=(
            P(None, "fsdp", "ctx", None),
            P(None, "fsdp", "ctx", None),
            P(None, "fsdp", None),
            P("fsdp", None),
        ),
        out_specs=P(None, "fsdp", "ctx", None),
        check_vma=False,
    )
```

profile of v0, /device:TPU:1, one launch (start us, length us, event | category | flops | bytes accessed | tf_op | source)
XLA Modules:
  0.0 606.8 jit_solution(2353301830229139808)
XLA Ops:
  6.5 0.7 all-gather.4.cloned.1.call-update
  7.3 199.6 %all-gather.4.cloned.1.call-done = bf16[2,3584,256]{2,1,0:T(8,128)(2,1)} async-done(((bf16[2,224,256]{2,1,0:T(8,128)(2,1)}), bf16[2,3584,256]{2,1,0:T(8,128)(2,1)}) %all-gather.4.cloned.1.call-update) | async-done | bytes 3670032 | tf_op jit(solution)/shard_map/all_gather | solution.py:128
  206.9 2.7 fusion.35
  214.5 1.9 broadcast_compare_fusion
  217.3 179.8 %all-gather.8.cloned.1.call-done = bf16[4096,2,128]{2,0,1:T(8,128)(2,1)} async-done(((bf16[64,2,128]{2,0,1:T(8,128)(2,1)}), bf16[4096,2,128]{2,0,1:T(8,128)(2,1)}) %all-gather.8.cloned.1.call-update) | async-done | bytes 2097168 | tf_op jit(solution)/shard_map/all_gather | solution.py:138
  397.1 160.5 %all-gather.6.cloned.1.call-done = bf16[4096,2,128]{2,0,1:T(8,128)(2,1)} async-done(((bf16[64,2,128]{2,0,1:T(8,128)(2,1)}), bf16[4096,2,128]{2,0,1:T(8,128)(2,1)}) %all-gather.6.cloned.1.call-update) | async-done | bytes 2097168 | tf_op jit(solution)/shard_map/all_gather | solution.py:137
  557.6 40.7 %while.17 = (s32[]{:T(128)}, f32[2,7,128]{2,1,0:T(8,128)S(1)}, f32[2,7,128]{2,1,0:T(8,128)S(1)}, f32[2,7,128,128]{3,2,1,0:T(8,128)S(1)}, pred[128,4096]{0,1:T(8,...) while((s32[]{:T(128)}, f32[2,7,128]{2,1,0:T(8,128)S(1)}, ...), condition=%wide.region_5.6_spmd, body=%wide.region_2.5_spmd.sunk | while | flops 482151936 | bytes 14270639 | solution.py:68
  557.6 1.6 fusion.49
  559.3 0.9 fusion.50
  560.2 2.5 fusion.51
  562.7 1.6 fusion.49
  564.4 0.9 fusion.50
  565.3 2.5 fusion.51
  567.8 1.6 fusion.49
  569.5 0.9 fusion.50
  570.4 2.5 fusion.51
  572.9 1.6 fusion.49
  574.6 0.9 fusion.50
  575.5 2.5 fusion.51
  578.0 1.6 fusion.49
  579.6 0.9 fusion.50
  580.6 2.5 fusion.51
  583.1 1.6 fusion.49
  584.7 0.9 fusion.50
  585.7 2.5 fusion.51
  588.2 1.6 fusion.49
  589.8 0.9 fusion.50
  590.7 2.5 fusion.51
  593.3 1.6 fusion.49
  594.9 0.9 fusion.50
  595.8 2.5 fusion.51
  599.0 1.3 convert_element_type.40
  (66 shorter events, 5.9 us)
Async XLA Ops:
  6.5 200.4 %copy-start = (bf16[2,1,64,3584]{3,2,1,0:T(8,128)(2,1)S(1)}, bf16[2,1,64,3584]{3,2,1,0:T(8,128)(2,1)}, u32[]{:S(2)}) copy-start(bf16[2,1,64,3584]{3,2,1,0:T(8,128)(2,1)} %param.6) | copy-start | bytes 2752516
  6.5 203.8 %copy-start.2 = (s32[1,64]{1,0:T(1,128)S(1)}, s32[1,64]{1,0:T(1,128)}, u32[]{:S(2)}) copy-start(s32[1,64]{1,0:T(1,128)} %param.9) | copy-start | bytes 772
  6.5 206.5 %copy-start.1 = (bf16[2,1,64,1792]{3,2,1,0:T(8,128)(2,1)S(1)}, bf16[2,1,64,1792]{3,2,1,0:T(8,128)(2,1)}, u32[]{:S(2)}) copy-start(bf16[2,1,64,1792]{3,2,1,0:T(8,128)(2,1)} %param.7) | copy-start | bytes 1376260
  6.5 200.4 %all-gather.4.cloned.1.call-start = ((), (), s32[]{:S(2)}) async-start(), calls=%async_computation | async-start | bytes 3899392 | tf_op jit(solution)/shard_map/all_gather | solution.py:128
  7.3 389.9 %all-gather.8.cloned.1.call-start = ((), (), s32[]{:S(2)}) async-start(), calls=%async_computation.2 | async-start | bytes 2129920 | tf_op jit(solution)/shard_map/all_gather | solution.py:138
  206.9 6.9 %copy-start.3 = (s32[128]{0:T(128)S(1)}, s32[128]{0:T(128)}, u32[]{:S(2)}) copy-start(s32[128]{0:T(128)} %constant.91.clone.1) | copy-start | bytes 1540
  210.3 347.4 %all-gather.6.cloned.1.call-start = ((), (), s32[]{:S(2)}) async-start(), calls=%async_computation.1 | async-start | bytes 2129920 | tf_op jit(solution)/shard_map/all_gather | solution.py:137
Sparse Core Ops, SparseCore 0:
  10.0 196.8 all-gather.3
  212.7 184.3 all-gather.7
  402.9 154.6 all-gather.5
where the time goes:
time: 607 us
  waiting for transfers between devices  541 us (89%)
  matrix products  36.4 us (6%)
  between operations  14 us (2%)
  other arithmetic  11.4 us (2%)
    all_gather x1, waiting for transfers between devices, local(): lax.all_gather(kv_panel, 'fsdp', axis=1, tiled=True)  200 us
    all_gather x1, waiting for transfers between devices, local(): lax.all_gather(value_rows[:block_len], 'ctx', axis=0, tiled=True)  180 us
    all_gather x1, waiting for transfers between devices, local(): lax.all_gather(key_rows[:block_len], 'ctx', axis=0, tiled=True)  160 us
    dot_general x9, matrix products, absorb(): jnp.einsum('gptu,ugd->gptd', weights.astype(jnp.bfloat16), value_part, pr...  20.2 us
    dot_general x9, matrix products, absorb(): jnp.einsum('tgpd,ugd->gptu', query_rows, key_part, preferred_element_type...  13.5 us
  transfers between devices with their start and end apart: 3, of which 3 were waited for; matrix products, arithmetic and copies ran while one was open for 1% of the time, Pallas kernels for 0%

commit v1 on v0

v1 whole, which is shorter than its diff:
```python
import math

import jax
import jax.numpy as jnp
from jax import lax
from jax.sharding import Mesh
from jax.sharding import PartitionSpec as P

NEGATIVE = -1e30
CTX = ("x", "y", "zh", "core")


def rotate_keys(vectors_in, positions, head_dim):
    half_dim = head_dim // 2
    inverse = 1000000.0 ** (-(jnp.arange(half_dim, dtype=jnp.float32) * 2.0 / head_dim))
    angles = positions.astype(jnp.float32)[..., None] * inverse
    cosine = jnp.cos(angles)
    sine_part = jnp.sin(angles)
    first_half = vectors_in[..., :half_dim]
    second_half = vectors_in[..., half_dim:]
    return jnp.concatenate(
        [
            first_half * cosine - second_half * sine_part,
            second_half * cosine + first_half * sine_part,
        ],
        axis=-1,
    )


def absorb(fold_carry, query_rows, key_part, value_part, allowed, score_scale):
    running, denominator, numerator = fold_carry
    scores = (
        jnp.einsum("tpd,ud->ptu", query_rows, key_part, preferred_element_type=jnp.float32)
        * score_scale
    )
    allowed_all = allowed[None]
    scores = jnp.where(allowed_all, scores, NEGATIVE)
    highest = jnp.maximum(running, jnp.max(scores, axis=-1))
    factor = jnp.exp(running - highest)
    weights = jnp.where(allowed_all, jnp.exp(scores - highest[..., None]), 0.0)
    denominator = denominator * factor + jnp.sum(weights, axis=-1)
    numerator = numerator * factor[..., None] + jnp.einsum(
        "ptu,ud->ptd",
        weights.astype(jnp.bfloat16),
        value_part,
        preferred_element_type=jnp.float32,
    )
    return (highest, denominator, numerator)


def absorb_tiled(fold_carry, query_rows, key_part, value_part, allowed, score_scale):
    key_count = key_part.shape[0]
    tile_width = math.gcd(key_count, 512)

    def one_tile(tile_index, inner):
        tile_start = tile_index * tile_width
        return absorb(
            inner,
            query_rows,
            lax.dynamic_slice_in_dim(key_part, tile_start, tile_width, 0),
            lax.dynamic_slice_in_dim(value_part, tile_start, tile_width, 0),
            lax.dynamic_slice_in_dim(allowed, tile_start, tile_width, 1),
            score_scale,
        )

    return lax.fori_loop(0, key_count // tile_width, one_tile, fold_carry)


def attend_block(query_rows, noisy_keys, noisy_values, clean_keys, clean_values, key_blocks,
                 own_block, block_len, score_scale):
    group_size = query_rows.shape[1]
    head_dim = query_rows.shape[2]
    rows_all = 2 * block_len
    fold_carry = (
        jnp.full((group_size, rows_all), NEGATIVE, jnp.float32),
        jnp.zeros((group_size, rows_all), jnp.float32),
        jnp.zeros((group_size, rows_all, head_dim), jnp.float32),
    )
    noisy_ok = jnp.broadcast_to((jnp.arange(rows_all) >= block_len)[:, None], (rows_all, block_len))
    fold_carry = absorb(fold_carry, query_rows, noisy_keys, noisy_values, noisy_ok, score_scale)
    block_limit = (
        jnp.concatenate([jnp.ones((block_len,), jnp.int32), jnp.zeros((block_len,), jnp.int32)])
        + own_block
    )
    key_block = jnp.repeat(key_blocks, block_len)
    allowed = key_block[None, :] < block_limit[:, None]
    fold_carry = absorb_tiled(fold_carry, query_rows, clean_keys, clean_values, allowed, score_scale)
    highest, denominator, numerator = fold_carry
    return jnp.transpose(numerator / denominator[..., None], (1, 0, 2))


def swap(value, axis):
    return lax.ppermute(value, axis, [(0, 1), (1, 0)])


def ring4(value, axis):
    size = 4
    forward = [(i, (i + 1) % size) for i in range(size)]
    backward = [(i, (i - 1) % size) for i in range(size)]
    from_left = lax.ppermute(value, axis, forward)
    from_right = lax.ppermute(value, axis, backward)
    from_left2 = lax.ppermute(from_left, axis, forward)
    return jnp.stack([value, from_left, from_left2, from_right])


RING_SHIFT = (0, -1, -2, 1)


def local(hidden, queries, kv_panel, layout):
    block_len = hidden.shape[2]
    model_width = hidden.shape[3]
    heads_kv = kv_panel.shape[0]
    chunk_rows = kv_panel.shape[1]
    head_dim = kv_panel.shape[2] // 2
    group_size = queries.shape[3] // (heads_kv * head_dim)
    group_width = group_size * head_dim
    score_scale = head_dim ** (-0.5)
    n_chunks = model_width // chunk_rows
    x = lax.axis_index("x")
    y = lax.axis_index("y")
    zh = lax.axis_index("zh")
    core = lax.axis_index("core")
    fsdp = lax.axis_index("fsdp")
    ctx = ((x * 4 + y) * 2 + zh) * 2 + core
    block_table = layout[0]

    z_size = 2 * n_chunks
    forward = [(z, (z + 1) % z_size) for z in range(z_size)]
    backward = [(z, (z - 1) % z_size) for z in range(z_size)]
    mine = lax.dynamic_index_in_dim(kv_panel, core, 0, keepdims=False)
    panel = jnp.zeros((n_chunks,) + mine.shape, mine.dtype)
    panel = lax.dynamic_update_index_in_dim(panel, mine, fsdp, 0)
    going_up = mine
    going_down = mine
    for step in range(1, n_chunks // 2 + 1):
        going_up = lax.ppermute(going_up, ("zh", "fsdp"), forward)
        panel = lax.dynamic_update_index_in_dim(panel, going_up, (fsdp - step) % n_chunks, 0)
        if step < n_chunks // 2:
            going_down = lax.ppermute(going_down, ("zh", "fsdp"), backward)
            panel = lax.dynamic_update_index_in_dim(
                panel, going_down, (fsdp + step) % n_chunks, 0
            )
    panel = panel.reshape(model_width, 2 * head_dim)

    own_rows = hidden.reshape(2, block_len, model_width)
    token_rows = jnp.stack([own_rows, swap(own_rows, "core")])
    own_queries = queries.reshape(2, block_len, heads_kv, group_width)
    query_mine = lax.dynamic_index_in_dim(own_queries, core, 2, keepdims=False)
    query_other = lax.dynamic_index_in_dim(own_queries, 1 - core, 2, keepdims=False)
    query_blocks = jnp.stack([query_mine, swap(query_other, "core")])
    ctx_blocks = jnp.stack([ctx, ctx + 1 - 2 * core])
    own_blocks = block_table[ctx_blocks]

    projected = jnp.einsum(
        "bctd,de->bcte", token_rows, panel, preferred_element_type=jnp.float32
    )
    positions = own_blocks[:, None] * block_len + jnp.arange(block_len, dtype=jnp.int32)
    key_rows = rotate_keys(projected[..., :head_dim], positions[:, None, :], head_dim).astype(
        jnp.bfloat16
    )
    value_rows = projected[..., head_dim:].astype(jnp.bfloat16)

    clean = jnp.concatenate([key_rows[:, 0], value_rows[:, 0]], axis=-1)
    gathered = jnp.stack([clean, swap(clean, "zh")])
    gathered = ring4(gathered, "x")
    gathered = ring4(gathered, "y")
    gathered = gathered.reshape(-1, 2 * head_dim)
    shifts = jnp.array(RING_SHIFT, jnp.int32)
    src_y = (y + shifts)[:, None, None, None] % 4
    src_x = (x + shifts)[None, :, None, None] % 4
    src_zh = (zh + jnp.arange(2))[None, None, :, None] % 2
    src_core = (core + jnp.arange(2))[None, None, None, :] % 2
    src = ((src_x * 4 + src_y) * 2 + src_zh) * 2 + src_core
    key_blocks = block_table[src.reshape(-1)]
    clean_keys = gathered[:, :head_dim]
    clean_values = gathered[:, head_dim:]

    query_rows = query_blocks.reshape(2, 2 * block_len, group_size, head_dim)
    attended = jax.vmap(
        lambda q, nk, nv, b: attend_block(
            q, nk, nv, clean_keys, clean_values, key_blocks, b, block_len, score_scale
        )
    )(query_rows, key_rows[:, 1], value_rows[:, 1], own_blocks)
    attended = attended.astype(jnp.bfloat16).reshape(2, 2, block_len, group_width)
    returned = swap(attended[1], "core")
    first = jnp.where(core == 0, attended[0], returned)
    second = jnp.where(core == 0, returned, attended[0])
    result = jnp.concatenate([first, second], axis=-1)
    return result.reshape(2, 1, block_len, heads_kv * group_width)


def solution(mesh):
    axis_sizes = dict(zip(mesh.axis_names, mesh.devices.shape))
    assert axis_sizes["ctx"] == 64
    fine = Mesh(mesh.devices.reshape(4, 4, 2, 2, axis_sizes["fsdp"]), CTX + ("fsdp",))
    return jax.shard_map(
        local,
        mesh=fine,
        in_specs=(
            P(None, "fsdp", CTX, None),
            P(None, "fsdp", CTX, None),
            P(None, "fsdp", None),
            P("fsdp", None),
        ),
        out_specs=P(None, "fsdp", CTX, None),
        check_vma=False,
    )
```

time: 607 us -> 219 us (0.36)
  waiting for transfers between devices: 541 us -> 44.3 us
  starting transfers between devices: 0.08 us -> 113 us
  local copies, waits for them, and re-layouts: 3.78 us -> 19.3 us
  between operations: 14 us -> 1.11 us
  matrix products: 36.4 us -> 27.9 us
    all_gather x3 -> x0, waiting for transfers between devices: 540 us -> none  [the longest x1 200 us: local(): lax.all_gather(kv_panel, 'fsdp', axis=1, tiled=True)]
    ppermute x0 -> x25, starting transfers between devices: none -> 113 us  [the longest x7 48.3 us: local(): going_down = lax.ppermute(going_down, ('zh', 'fsdp'), backward)]
    ppermute x0 -> x25, waiting for transfers between devices: none -> 44.3 us  [the longest x2 17.3 us: ring4(): from_left2 = lax.ppermute(from_left, axis, forward)]
    while x8 -> x24, local copies, waits for them, and re-layouts: 0.02 us -> 11.6 us  [the longest x16 11.6 us: one_tile(): lax.dynamic_slice_in_dim(allowed, tile_start, tile_width, 1)]
    dot_general x19, matrix products: 36.4 us -> 27.9 us  [the longest x9 19.9 us: absorb(): jnp.einsum('ptu,ud->ptd', weights.astype(jnp.bfloat16), value_part, prefe...]
  transfers between devices with their start and end apart: 3 -> 25, of which waited for: 3 -> 7; matrix products, arithmetic and copies ran while one was open for 1% -> 5% of each run, Pallas kernels for 0% -> 0%
where the time goes in v1:
time: 219 us; the launch traced here: 218 us
  starting transfers between devices  113 us (52%)
  waiting for transfers between devices  44.3 us (20%)
  matrix products  27.9 us (13%)
  local copies, waits for them, and re-layouts  19.3 us (9%)
  other arithmetic  12.3 us (6%)
    ppermute x7, starting transfers between devices, local(): going_down = lax.ppermute(going_down, ('zh', 'fsdp'), backward)  48.3 us
    ppermute x4, starting transfers between devices, swap(): return lax.ppermute(value, axis, [(0, 1), (1, 0)])  32 us
    dot_general x9, matrix products, absorb(): jnp.einsum('ptu,ud->ptd', weights.astype(jnp.bfloat16), value_part, prefe...  19.9 us
    ppermute x2, waiting for transfers between devices, ring4(): from_left2 = lax.ppermute(from_left, axis, forward)  17.3 us
    ppermute x8, starting transfers between devices, local(): going_up = lax.ppermute(going_up, ('zh', 'fsdp'), forward)  15.3 us
    ppermute x4, waiting for transfers between devices, swap(): return lax.ppermute(value, axis, [(0, 1), (1, 0)])  11.7 us
    while x16, local copies, waits for them, and re-layouts, one_tile(): lax.dynamic_slice_in_dim(allowed, tile_start, tile_width, 1)  11.6 us
    ppermute x8, waiting for transfers between devices, local(): going_up = lax.ppermute(going_up, ('zh', 'fsdp'), forward)  11 us
  transfers between devices with their start and end apart: 25, of which 7 were waited for; matrix products, arithmetic and copies ran while one was open for 5% of the time, Pallas kernels for 0%

profile of v1, /device:TPU:1, one launch (start us, length us, event | category | flops | bytes accessed | tf_op | source)
XLA Modules:
  0.0 218.3 jit_solution(8343271231703247721)
XLA Ops:
  1.0 19.2 %collective-permute-start.2 = (bf16[224,256]{1,0:T(8,128)(2,1)S(1)}, bf16[224,256]{1,0:T(8,128)(2,1)S(1)}, u32[]{:S(2)}, u32[]{:S(2)}) collective-permute-start(bf16[224,256]{1,0:T(8,128)(2,1)S(1)} %get-tuple-element.192), channel_id=1, source_target_pairs={{0,47},{1,0},{2,1},{3,2},{4,3},{5,4},{6,5},{7,6},{8,7},{9,8},{10,9... | collective-permute-start | bytes 344072 | tf_op jit(solution)/shard_map/ppermute | solution.py:139
  24.2 2.9 %collective-permute-start.16 = (bf16[2,64,896]{2,1,0:T(8,128)(2,1)S(1)}, bf16[2,64,896]{2,1,0:T(8,128)(2,1)S(1)}, u32[]{:S(2)}, u32[]{:S(2)}) collective-permute-start(bf16[2,64,896]{2,1,0:T(8,128)(2,1)S(1)} %bitcast.149), channel_id=1, source_target_pairs={{0,16},{16,0},{1,17},{17,1},{2,18},{18,2},{3,19},{19,3},{4,20},{20... | collective-permute-start | bytes 688136 | tf_op jit(solution)/shard_map/ppermute | solution.py:93
  27.1 1.9 collective-permute-start
  31.0 4.9 %collective-permute-start.4 = (bf16[224,256]{1,0:T(8,128)(2,1)S(1)}, bf16[224,256]{1,0:T(8,128)(2,1)S(1)}, u32[]{:S(2)}, u32[]{:S(2)}) collective-permute-start(bf16[224,256]{1,0:T(8,128)(2,1)S(1)} %collective-permute-done.2), channel_id=1, source_target_pairs={{0,47},{1,0},{2,1},{3,2},{4,3},{5,4},{6,5},{7,6},{8,7},{9,8},{10,9... | collective-permute-start | bytes 344072 | tf_op jit(solution)/shard_map/ppermute | solution.py:139
  37.9 5.3 %collective-permute-start.6 = (bf16[224,256]{1,0:T(8,128)(2,1)S(1)}, bf16[224,256]{1,0:T(8,128)(2,1)S(1)}, u32[]{:S(2)}, u32[]{:S(2)}) collective-permute-start(bf16[224,256]{1,0:T(8,128)(2,1)S(1)} %collective-permute-done.4), channel_id=1, source_target_pairs={{0,47},{1,0},{2,1},{3,2},{4,3},{5,4},{6,5},{7,6},{8,7},{9,8},{10,9... | collective-permute-start | bytes 344072 | tf_op jit(solution)/shard_map/ppermute | solution.py:139
  45.2 4.7 %collective-permute-start.8 = (bf16[224,256]{1,0:T(8,128)(2,1)S(1)}, bf16[224,256]{1,0:T(8,128)(2,1)S(1)}, u32[]{:S(2)}, u32[]{:S(2)}) collective-permute-start(bf16[224,256]{1,0:T(8,128)(2,1)S(1)} %collective-permute-done.6), channel_id=1, source_target_pairs={{0,47},{1,0},{2,1},{3,2},{4,3},{5,4},{6,5},{7,6},{8,7},{9,8},{10,9... | collective-permute-start | bytes 344072 | tf_op jit(solution)/shard_map/ppermute | solution.py:139
  51.9 4.7 %collective-permute-start.10 = (bf16[224,256]{1,0:T(8,128)(2,1)S(1)}, bf16[224,256]{1,0:T(8,128)(2,1)S(1)}, u32[]{:S(2)}, u32[]{:S(2)}) collective-permute-start(bf16[224,256]{1,0:T(8,128)(2,1)S(1)} %collective-permute-done.8), channel_id=1, source_target_pairs={{0,47},{1,0},{2,1},{3,2},{4,3},{5,4},{6,5},{7,6},{8,7},{9,8},{10,9... | collective-permute-start | bytes 344072 | tf_op jit(solution)/shard_map/ppermute | solution.py:139
  58.6 4.7 %collective-permute-start.12 = (bf16[224,256]{1,0:T(8,128)(2,1)S(1)}, bf16[224,256]{1,0:T(8,128)(2,1)S(1)}, u32[]{:S(2)}, u32[]{:S(2)}) collective-permute-start(bf16[224,256]{1,0:T(8,128)(2,1)S(1)} %collective-permute-done.10), channel_id=1, source_target_pairs={{0,47},{1,0},{2,1},{3,2},{4,3},{5,4},{6,5},{7,6},{8,7},{9,8},{10,9... | collective-permute-start | bytes 344072 | tf_op jit(solution)/shard_map/ppermute | solution.py:139
  65.4 4.7 %collective-permute-start.14 = (bf16[224,256]{1,0:T(8,128)(2,1)S(1)}, bf16[224,256]{1,0:T(8,128)(2,1)S(1)}, u32[]{:S(2)}, u32[]{:S(2)}) collective-permute-start(bf16[224,256]{1,0:T(8,128)(2,1)S(1)} %collective-permute-done.12), channel_id=1, source_target_pairs={{0,47},{1,0},{2,1},{3,2},{4,3},{5,4},{6,5},{7,6},{8,7},{9,8},{10,9... | collective-permute-start | bytes 344072 | tf_op jit(solution)/shard_map/ppermute | solution.py:139
  72.1 4.8 %collective-permute-done.13 = bf16[224,256]{1,0:T(8,128)(2,1)S(1)} collective-permute-done((bf16[224,256]{1,0:T(8,128)(2,1)S(1)}, bf16[224,256]{1,0:T(8,128)(2,1)S(1)}, u32[]{:S(2)}, u32[]{:S(2)}) %collective-permute-start.13) | collective-permute-done | bytes 114720 | tf_op jit(solution)/shard_map/ppermute | solution.py:136
  78.9 6.1 %collective-permute-done.15 = bf16[224,256]{1,0:T(8,128)(2,1)S(1)} collective-permute-done((bf16[224,256]{1,0:T(8,128)(2,1)S(1)}, bf16[224,256]{1,0:T(8,128)(2,1)S(1)}, u32[]{:S(2)}, u32[]{:S(2)}) %collective-permute-start.15) | collective-permute-done | bytes 114720 | tf_op jit(solution)/shard_map/ppermute | solution.py:136
  85.0 2.1 fusion.53
  87.4 12.0 %collective-permute-start.17 = (bf16[2,64,256]{2,1,0:T(8,128)(2,1)S(1)}, bf16[2,64,256]{2,1,0:T(8,128)(2,1)S(1)}, u32[]{:S(2)}, u32[]{:S(2)}) collective-permute-start(bf16[2,64,256]{2,1,0:T(8,128)(2,1)S(1)} %get-tuple-element.197), channel_id=1, source_target_pairs={{0,32},{32,0},{1,33},{33,1},{2,34},{34,2},{3,35},{35,3},{4,36},{36... | collective-permute-start | bytes 196616 | tf_op jit(solution)/shard_map/ppermute | solution.py:93
  100.4 11.1 %collective-permute-done.17 = bf16[2,64,256]{2,1,0:T(8,128)(2,1)S(1)} collective-permute-done((bf16[2,64,256]{2,1,0:T(8,128)(2,1)S(1)}, bf16[2,64,256]{2,1,0:T(8,128)(2,1)S(1)}, u32[]{:S(2)}, u32[]{:S(2)}) %collective-permute-start.17) | collective-permute-done | bytes 65568 | tf_op jit(solution)/shard_map/ppermute | solution.py:93
  111.5 3.1 %collective-permute-start.18 = (bf16[2,2,64,256]{3,2,1,0:T(8,128)(2,1)S(1)}, bf16[2,2,64,256]{3,2,1,0:T(8,128)(2,1)S(1)}, u32[]{:S(2)}, u32[]{:S(2)}) collective-permute-start(bf16[2,2,64,256]{3,2,1,0:T(8,128)(2,1)S(1)} %get-tuple-element.195), channel_id=1, source_target_pairs={{0,256},{256,512},{512,768},{768,0},{1,257},{257,513},{513,769},{7... | collective-permute-start | bytes 393224 | tf_op jit(solution)/shard_map/ppermute | solution.py:100
  116.8 3.4 %collective-permute-start.20 = (bf16[2,2,64,256]{3,2,1,0:T(8,128)(2,1)S(1)}, bf16[2,2,64,256]{3,2,1,0:T(8,128)(2,1)S(1)}, u32[]{:S(2)}, u32[]{:S(2)}) collective-permute-start(bf16[2,2,64,256]{3,2,1,0:T(8,128)(2,1)S(1)} %get-tuple-element.195), channel_id=1, source_target_pairs={{0,768},{256,0},{512,256},{768,512},{1,769},{257,1},{513,257},{769... | collective-permute-start | bytes 393224 | tf_op jit(solution)/shard_map/ppermute | solution.py:101
  122.5 4.6 %collective-permute-done.19 = bf16[2,2,64,256]{3,2,1,0:T(8,128)(2,1)S(1)} collective-permute-done((bf16[2,2,64,256]{3,2,1,0:T(8,128)(2,1)S(1)}, bf16[2,2,64,256]{3,2,1,0:T(8,128)(2,1)S(1)}, u32[]{:S(2)}, u32[]{:S(2)}) %collective-permute-start.19) | collective-permute-done | bytes 131104 | tf_op jit(solution)/shard_map/ppermute | solution.py:102
  127.2 3.2 %collective-permute-start.21 = (bf16[4,2,2,64,256]{4,3,2,1,0:T(8,128)(2,1)S(1)}, bf16[4,2,2,64,256]{4,3,2,1,0:T(8,128)(2,1)S(1)}, u32[]{:S(2)}, u32[]{:S(2)}) collective-permute-start(bf16[4,2,2,64,256]{4,3,2,1,0:T(8,128)(2,1)S(1)} %get-tuple-element.181), channel_id=1, source_target_pairs={{0,64},{64,128},{128,192},{192,0},{1,65},{65,129},{129,193},{193,1... | collective-permute-start | bytes 1572872 | tf_op jit(solution)/shard_map/ppermute | solution.py:100
  130.8 3.4 %collective-permute-start.23 = (bf16[4,2,2,64,256]{4,3,2,1,0:T(8,128)(2,1)S(1)}, bf16[4,2,2,64,256]{4,3,2,1,0:T(8,128)(2,1)S(1)}, u32[]{:S(2)}, u32[]{:S(2)}) collective-permute-start(bf16[4,2,2,64,256]{4,3,2,1,0:T(8,128)(2,1)S(1)} %get-tuple-element.181), channel_id=1, source_target_pairs={{0,192},{64,0},{128,64},{192,128},{1,193},{65,1},{129,65},{193,129... | collective-permute-start | bytes 1572872 | tf_op jit(solution)/shard_map/ppermute | solution.py:101
  134.2 4.2 %collective-permute-done.21 = bf16[4,2,2,64,256]{4,3,2,1,0:T(8,128)(2,1)S(1)} collective-permute-done((bf16[4,2,2,64,256]{4,3,2,1,0:T(8,128)(2,1)S(1)}, bf16[4,2,2,64,256]{4,3,2,1,0:T(8,128)(2,1)S(1)}, u32[]{:S(2)}, u32[]{:S(2)}) %collective-permute-start.21) | collective-permute-done | bytes 524320 | tf_op jit(solution)/shard_map/ppermute | solution.py:100
  138.4 2.4 %collective-permute-start.22 = (bf16[4,2,2,64,256]{4,3,2,1,0:T(8,128)(2,1)S(1)}, bf16[4,2,2,64,256]{4,3,2,1,0:T(8,128)(2,1)S(1)}, u32[]{:S(2)}, u32[]{:S(2)}) collective-permute-start(bf16[4,2,2,64,256]{4,3,2,1,0:T(8,128)(2,1)S(1)} %collective-permute-done.21), channel_id=1, source_target_pairs={{0,64},{64,128},{128,192},{192,0},{1,65},{65,129},{129,193},{193,1... | collective-permute-start | bytes 1572872 | tf_op jit(solution)/shard_map/ppermute | solution.py:102
  142.2 12.7 %collective-permute-done.22 = bf16[4,2,2,64,256]{4,3,2,1,0:T(8,128)(2,1)S(1)} collective-permute-done((bf16[4,2,2,64,256]{4,3,2,1,0:T(8,128)(2,1)S(1)}, bf16[4,2,2,64,256]{4,3,2,1,0:T(8,128)(2,1)S(1)}, u32[]{:S(2)}, u32[]{:S(2)}) %collective-permute-start.22) | collective-permute-done | bytes 524320 | tf_op jit(solution)/shard_map/ppermute | solution.py:102
  156.2 44.2 %while.18 = (s32[]{:T(128)}, f32[2,7,128]{2,1,0:T(8,128)S(1)}, f32[2,7,128]{2,1,0:T(8,128)S(1)}, f32[2,7,128,128]{3,2,1,0:T(8,128)S(1)}, pred[2,128,4096]{1,2,0:...) while((s32[]{:T(128)}, f32[2,7,128]{2,1,0:T(8,128)S(1)}, ...), condition=%wide.region_5.6_spmd, body=%wide.region_2.5_spmd.sunk | while | flops 482151936 | bytes 14336715 | solution.py:66
  159.3 2.3 %fusion.69 = f32[2,7,128,128]{3,2,1,0:T(8,128)S(1)} fusion(f32[512,2,128,7]{2,0,3,1:T(8,128)S(1)} %get-tuple-element.264, f32[2,7,128]{2,1,0:T(8,128)S(1)} %max.8, pred[2,128,512]{1,2,0:T(8,128)(4,1)S(1)} %constant_dynamic-slice_fusion.3, f32[2,7,128,128]{3,2,1,0:T(8,128)S(1)} %get-tuple-element.283, f32[2,7,128]{2,1,0:T(8,128)S(1)} %get-tuple-element.266, ...), kind=kOutput, calls=%fused_computation.9.clone.1 | convolution fusion | flops 239927296 | bytes 5782016 | tf_op jit(solution)/shard_map/vmap()/while/body/eval_jaxpr/ptu,ud->ptd/dot_general | solution.py:42
  164.9 2.3 %fusion.69 = f32[2,7,128,128]{3,2,1,0:T(8,128)S(1)} fusion(f32[512,2,128,7]{2,0,3,1:T(8,128)S(1)} %get-tuple-element.264, f32[2,7,128]{2,1,0:T(8,128)S(1)} %max.8, pred[2,128,512]{1,2,0:T(8,128)(4,1)S(1)} %constant_dynamic-slice_fusion.3, f32[2,7,128,128]{3,2,1,0:T(8,128)S(1)} %get-tuple-element.283, f32[2,7,128]{2,1,0:T(8,128)S(1)} %get-tuple-element.266, ...), kind=kOutput, calls=%fused_computation.9.clone.1 | convolution fusion | flops 239927296 | bytes 5782016 | tf_op jit(solution)/shard_map/vmap()/while/body/eval_jaxpr/ptu,ud->ptd/dot_general | solution.py:42
  170.4 2.3 %fusion.69 = f32[2,7,128,128]{3,2,1,0:T(8,128)S(1)} fusion(f32[512,2,128,7]{2,0,3,1:T(8,128)S(1)} %get-tuple-element.264, f32[2,7,128]{2,1,0:T(8,128)S(1)} %max.8, pred[2,128,512]{1,2,0:T(8,128)(4,1)S(1)} %constant_dynamic-slice_fusion.3, f32[2,7,128,128]{3,2,1,0:T(8,128)S(1)} %get-tuple-element.283, f32[2,7,128]{2,1,0:T(8,128)S(1)} %get-tuple-element.266, ...), kind=kOutput, calls=%fused_computation.9.clone.1 | convolution fusion | flops 239927296 | bytes 5782016 | tf_op jit(solution)/shard_map/vmap()/while/body/eval_jaxpr/ptu,ud->ptd/dot_general | solution.py:42
  175.9 2.3 %fusion.69 = f32[2,7,128,128]{3,2,1,0:T(8,128)S(1)} fusion(f32[512,2,128,7]{2,0,3,1:T(8,128)S(1)} %get-tuple-element.264, f32[2,7,128]{2,1,0:T(8,128)S(1)} %max.8, pred[2,128,512]{1,2,0:T(8,128)(4,1)S(1)} %constant_dynamic-slice_fusion.3, f32[2,7,128,128]{3,2,1,0:T(8,128)S(1)} %get-tuple-element.283, f32[2,7,128]{2,1,0:T(8,128)S(1)} %get-tuple-element.266, ...), kind=kOutput, calls=%fused_computation.9.clone.1 | convolution fusion | flops 239927296 | bytes 5782016 | tf_op jit(solution)/shard_map/vmap()/while/body/eval_jaxpr/ptu,ud->ptd/dot_general | solution.py:42
  181.5 2.3 %fusion.69 = f32[2,7,128,128]{3,2,1,0:T(8,128)S(1)} fusion(f32[512,2,128,7]{2,0,3,1:T(8,128)S(1)} %get-tuple-element.264, f32[2,7,128]{2,1,0:T(8,128)S(1)} %max.8, pred[2,128,512]{1,2,0:T(8,128)(4,1)S(1)} %constant_dynamic-slice_fusion.3, f32[2,7,128,128]{3,2,1,0:T(8,128)S(1)} %get-tuple-element.283, f32[2,7,128]{2,1,0:T(8,128)S(1)} %get-tuple-element.266, ...), kind=kOutput, calls=%fused_computation.9.clone.1 | convolution fusion | flops 239927296 | bytes 5782016 | tf_op jit(solution)/shard_map/vmap()/while/body/eval_jaxpr/ptu,ud->ptd/dot_general | solution.py:42
  187.0 2.3 %fusion.69 = f32[2,7,128,128]{3,2,1,0:T(8,128)S(1)} fusion(f32[512,2,128,7]{2,0,3,1:T(8,128)S(1)} %get-tuple-element.264, f32[2,7,128]{2,1,0:T(8,128)S(1)} %max.8, pred[2,128,512]{1,2,0:T(8,128)(4,1)S(1)} %constant_dynamic-slice_fusion.3, f32[2,7,128,128]{3,2,1,0:T(8,128)S(1)} %get-tuple-element.283, f32[2,7,128]{2,1,0:T(8,128)S(1)} %get-tuple-element.266, ...), kind=kOutput, calls=%fused_computation.9.clone.1 | convolution fusion | flops 239927296 | bytes 5782016 | tf_op jit(solution)/shard_map/vmap()/while/body/eval_jaxpr/ptu,ud->ptd/dot_general | solution.py:42
  192.5 2.3 %fusion.69 = f32[2,7,128,128]{3,2,1,0:T(8,128)S(1)} fusion(f32[512,2,128,7]{2,0,3,1:T(8,128)S(1)} %get-tuple-element.264, f32[2,7,128]{2,1,0:T(8,128)S(1)} %max.8, pred[2,128,512]{1,2,0:T(8,128)(4,1)S(1)} %constant_dynamic-slice_fusion.3, f32[2,7,128,128]{3,2,1,0:T(8,128)S(1)} %get-tuple-element.283, f32[2,7,128]{2,1,0:T(8,128)S(1)} %get-tuple-element.266, ...), kind=kOutput, calls=%fused_computation.9.clone.1 | convolution fusion | flops 239927296 | bytes 5782016 | tf_op jit(solution)/shard_map/vmap()/while/body/eval_jaxpr/ptu,ud->ptd/dot_general | solution.py:42
  198.1 2.3 %fusion.69 = f32[2,7,128,128]{3,2,1,0:T(8,128)S(1)} fusion(f32[512,2,128,7]{2,0,3,1:T(8,128)S(1)} %get-tuple-element.264, f32[2,7,128]{2,1,0:T(8,128)S(1)} %max.8, pred[2,128,512]{1,2,0:T(8,128)(4,1)S(1)} %constant_dynamic-slice_fusion.3, f32[2,7,128,128]{3,2,1,0:T(8,128)S(1)} %get-tuple-element.283, f32[2,7,128]{2,1,0:T(8,128)S(1)} %get-tuple-element.266, ...), kind=kOutput, calls=%fused_computation.9.clone.1 | convolution fusion | flops 239927296 | bytes 5782016 | tf_op jit(solution)/shard_map/vmap()/while/body/eval_jaxpr/ptu,ud->ptd/dot_general | solution.py:42
  201.3 15.1 %collective-permute-start.24 = (bf16[2,64,896]{2,1,0:T(8,128)(2,1)S(1)}, bf16[2,64,896]{2,1,0:T(8,128)(2,1)S(1)}, u32[]{:S(2)}, u32[]{:S(2)}) collective-permute-start(bf16[2,64,896]{2,1,0:T(8,128)(2,1)S(1)} %squeeze.39), channel_id=1, source_target_pairs={{0,16},{16,0},{1,17},{17,1},{2,18},{18,2},{3,19},{19,3},{4,20},{20... | collective-permute-start | bytes 688136 | tf_op jit(solution)/shard_map/ppermute | solution.py:93
  (171 shorter events, 56.7 us)
Async XLA Ops:
  0.0 29.4 %copy-start = (s32[1,64]{1,0:T(1,128)S(1)}, s32[1,64]{1,0:T(1,128)}, u32[]{:S(2)}) copy-start(s32[1,64]{1,0:T(1,128)} %param.10) | copy-start | bytes 772
  0.0 1.0 copy-start.2
  0.0 22.1 %copy-start.1 = (bf16[2,1,64,1792]{3,2,1,0:T(8,128)(2,1)S(1)}, bf16[2,1,64,1792]{3,2,1,0:T(8,128)(2,1)}, u32[]{:S(2)}) copy-start(bf16[2,1,64,1792]{3,2,1,0:T(8,128)(2,1)} %param.8) | copy-start | bytes 1376260
  1.0 30.0 %collective-permute-start.2 = (bf16[224,256]{1,0:T(8,128)(2,1)S(1)}, bf16[224,256]{1,0:T(8,128)(2,1)S(1)}, u32[]{:S(2)}, u32[]{:S(2)}) collective-permute-start(bf16[224,256]{1,0:T(8,128)(2,1)S(1)} %get-tuple-element.192), channel_id=1, source_target_pairs={{0,47},{1,0},{2,1},{3,2},{4,3},{5,4},{6,5},{7,6},{8,7},{9,8},{10,9... | collective-permute-start | bytes 344072 | tf_op jit(solution)/shard_map/ppermute | solution.py:139
  20.2 15.7 %collective-permute-start.1 = (bf16[224,256]{1,0:T(8,128)(2,1)S(1)}, bf16[224,256]{1,0:T(8,128)(2,1)S(1)}, u32[]{:S(2)}, u32[]{:S(2)}) collective-permute-start(bf16[224,256]{1,0:T(8,128)(2,1)S(1)} %get-tuple-element.192), channel_id=1, source_target_pairs={{0,1},{1,2},{2,3},{3,4},{4,5},{5,6},{6,7},{7,8},{8,9},{9,10},{10,1... | collective-permute-start | bytes 344072 | tf_op jit(solution)/shard_map/ppermute | solution.py:136
  22.1 7.2 %copy-start.4 = (s32[4]{0:T(128)S(1)}, s32[4]{0:T(128)}, u32[]{:S(2)}) copy-start(s32[4]{0:T(128)} %constant.300.clone) | copy-start | bytes 52
  22.3 7.8 %copy-start.5 = (s32[128]{0:T(128)S(1)}, s32[128]{0:T(128)}, u32[]{:S(2)}) copy-start(s32[128]{0:T(128)} %constant.299.clone.1) | copy-start | bytes 1540
  24.2 97.9 %collective-permute-start.16 = (bf16[2,64,896]{2,1,0:T(8,128)(2,1)S(1)}, bf16[2,64,896]{2,1,0:T(8,128)(2,1)S(1)}, u32[]{:S(2)}, u32[]{:S(2)}) collective-permute-start(bf16[2,64,896]{2,1,0:T(8,128)(2,1)S(1)} %bitcast.149), channel_id=1, source_target_pairs={{0,16},{16,0},{1,17},{17,1},{2,18},{18,2},{3,19},{19,3},{4,20},{20... | collective-permute-start | bytes 688136 | tf_op jit(solution)/shard_map/ppermute | solution.py:93
  27.1 57.9 %collective-permute-start = (bf16[2,64,3584]{2,1,0:T(8,128)(2,1)}, bf16[2,64,3584]{2,1,0:T(8,128)(2,1)}, u32[]{:S(2)}, u32[]{:S(2)}) collective-permute-start(bf16[2,64,3584]{2,1,0:T(8,128)(2,1)} %bitcast.9), channel_id=1, source_target_pairs={{0,16},{16,0},{1,17},{17,1},{2,18},{18,2},{3,19},{19,3},{4,20},{20... | collective-permute-start | bytes 2752520 | tf_op jit(solution)/shard_map/ppermute | solution.py:93
  31.0 6.8 %collective-permute-start.4 = (bf16[224,256]{1,0:T(8,128)(2,1)S(1)}, bf16[224,256]{1,0:T(8,128)(2,1)S(1)}, u32[]{:S(2)}, u32[]{:S(2)}) collective-permute-start(bf16[224,256]{1,0:T(8,128)(2,1)S(1)} %collective-permute-done.2), channel_id=1, source_target_pairs={{0,47},{1,0},{2,1},{3,2},{4,3},{5,4},{6,5},{7,6},{8,7},{9,8},{10,9... | collective-permute-start | bytes 344072 | tf_op jit(solution)/shard_map/ppermute | solution.py:139
  35.9 7.3 %collective-permute-start.3 = (bf16[224,256]{1,0:T(8,128)(2,1)S(1)}, bf16[224,256]{1,0:T(8,128)(2,1)S(1)}, u32[]{:S(2)}, u32[]{:S(2)}) collective-permute-start(bf16[224,256]{1,0:T(8,128)(2,1)S(1)} %collective-permute-done.1), channel_id=1, source_target_pairs={{0,1},{1,2},{2,3},{3,4},{4,5},{5,6},{6,7},{7,8},{8,9},{9,10},{10,1... | collective-permute-start | bytes 344072 | tf_op jit(solution)/shard_map/ppermute | solution.py:136
  37.9 7.3 %collective-permute-start.6 = (bf16[224,256]{1,0:T(8,128)(2,1)S(1)}, bf16[224,256]{1,0:T(8,128)(2,1)S(1)}, u32[]{:S(2)}, u32[]{:S(2)}) collective-permute-start(bf16[224,256]{1,0:T(8,128)(2,1)S(1)} %collective-permute-done.4), channel_id=1, source_target_pairs={{0,47},{1,0},{2,1},{3,2},{4,3},{5,4},{6,5},{7,6},{8,7},{9,8},{10,9... | collective-permute-start | bytes 344072 | tf_op jit(solution)/shard_map/ppermute | solution.py:139
  43.2 6.7 %collective-permute-start.5 = (bf16[224,256]{1,0:T(8,128)(2,1)S(1)}, bf16[224,256]{1,0:T(8,128)(2,1)S(1)}, u32[]{:S(2)}, u32[]{:S(2)}) collective-permute-start(bf16[224,256]{1,0:T(8,128)(2,1)S(1)} %collective-permute-done.3), channel_id=1, source_target_pairs={{0,1},{1,2},{2,3},{3,4},{4,5},{5,6},{6,7},{7,8},{8,9},{9,10},{10,1... | collective-permute-start | bytes 344072 | tf_op jit(solution)/shard_map/ppermute | solution.py:136
  45.2 6.7 %collective-permute-start.8 = (bf16[224,256]{1,0:T(8,128)(2,1)S(1)}, bf16[224,256]{1,0:T(8,128)(2,1)S(1)}, u32[]{:S(2)}, u32[]{:S(2)}) collective-permute-start(bf16[224,256]{1,0:T(8,128)(2,1)S(1)} %collective-permute-done.6), channel_id=1, source_target_pairs={{0,47},{1,0},{2,1},{3,2},{4,3},{5,4},{6,5},{7,6},{8,7},{9,8},{10,9... | collective-permute-start | bytes 344072 | tf_op jit(solution)/shard_map/ppermute | solution.py:139
  49.9 6.7 %collective-permute-start.7 = (bf16[224,256]{1,0:T(8,128)(2,1)S(1)}, bf16[224,256]{1,0:T(8,128)(2,1)S(1)}, u32[]{:S(2)}, u32[]{:S(2)}) collective-permute-start(bf16[224,256]{1,0:T(8,128)(2,1)S(1)} %collective-permute-done.5), channel_id=1, source_target_pairs={{0,1},{1,2},{2,3},{3,4},{4,5},{5,6},{6,7},{7,8},{8,9},{9,10},{10,1... | collective-permute-start | bytes 344072 | tf_op jit(solution)/shard_map/ppermute | solution.py:136
  51.9 6.7 %collective-permute-start.10 = (bf16[224,256]{1,0:T(8,128)(2,1)S(1)}, bf16[224,256]{1,0:T(8,128)(2,1)S(1)}, u32[]{:S(2)}, u32[]{:S(2)}) collective-permute-start(bf16[224,256]{1,0:T(8,128)(2,1)S(1)} %collective-permute-done.8), channel_id=1, source_target_pairs={{0,47},{1,0},{2,1},{3,2},{4,3},{5,4},{6,5},{7,6},{8,7},{9,8},{10,9... | collective-permute-start | bytes 344072 | tf_op jit(solution)/shard_map/ppermute | solution.py:139
  56.7 6.7 %collective-permute-start.9 = (bf16[224,256]{1,0:T(8,128)(2,1)S(1)}, bf16[224,256]{1,0:T(8,128)(2,1)S(1)}, u32[]{:S(2)}, u32[]{:S(2)}) collective-permute-start(bf16[224,256]{1,0:T(8,128)(2,1)S(1)} %collective-permute-done.7), channel_id=1, source_target_pairs={{0,1},{1,2},{2,3},{3,4},{4,5},{5,6},{6,7},{7,8},{8,9},{9,10},{10,1... | collective-permute-start | bytes 344072 | tf_op jit(solution)/shard_map/ppermute | solution.py:136
  58.6 6.7 %collective-permute-start.12 = (bf16[224,256]{1,0:T(8,128)(2,1)S(1)}, bf16[224,256]{1,0:T(8,128)(2,1)S(1)}, u32[]{:S(2)}, u32[]{:S(2)}) collective-permute-start(bf16[224,256]{1,0:T(8,128)(2,1)S(1)} %collective-permute-done.10), channel_id=1, source_target_pairs={{0,47},{1,0},{2,1},{3,2},{4,3},{5,4},{6,5},{7,6},{8,7},{9,8},{10,9... | collective-permute-start | bytes 344072 | tf_op jit(solution)/shard_map/ppermute | solution.py:139
  63.4 6.7 %collective-permute-start.11 = (bf16[224,256]{1,0:T(8,128)(2,1)S(1)}, bf16[224,256]{1,0:T(8,128)(2,1)S(1)}, u32[]{:S(2)}, u32[]{:S(2)}) collective-permute-start(bf16[224,256]{1,0:T(8,128)(2,1)S(1)} %collective-permute-done.9), channel_id=1, source_target_pairs={{0,1},{1,2},{2,3},{3,4},{4,5},{5,6},{6,7},{7,8},{8,9},{9,10},{10,1... | collective-permute-start | bytes 344072 | tf_op jit(solution)/shard_map/ppermute | solution.py:136
  65.4 13.5 %collective-permute-start.14 = (bf16[224,256]{1,0:T(8,128)(2,1)S(1)}, bf16[224,256]{1,0:T(8,128)(2,1)S(1)}, u32[]{:S(2)}, u32[]{:S(2)}) collective-permute-start(bf16[224,256]{1,0:T(8,128)(2,1)S(1)} %collective-permute-done.12), channel_id=1, source_target_pairs={{0,47},{1,0},{2,1},{3,2},{4,3},{5,4},{6,5},{7,6},{8,7},{9,8},{10,9... | collective-permute-start | bytes 344072 | tf_op jit(solution)/shard_map/ppermute | solution.py:139
  70.1 6.8 %collective-permute-start.13 = (bf16[224,256]{1,0:T(8,128)(2,1)S(1)}, bf16[224,256]{1,0:T(8,128)(2,1)S(1)}, u32[]{:S(2)}, u32[]{:S(2)}) collective-permute-start(bf16[224,256]{1,0:T(8,128)(2,1)S(1)} %collective-permute-done.11), channel_id=1, source_target_pairs={{0,1},{1,2},{2,3},{3,4},{4,5},{5,6},{6,7},{7,8},{8,9},{9,10},{10,1... | collective-permute-start | bytes 344072 | tf_op jit(solution)/shard_map/ppermute | solution.py:136
  76.9 8.1 %collective-permute-start.15 = (bf16[224,256]{1,0:T(8,128)(2,1)S(1)}, bf16[224,256]{1,0:T(8,128)(2,1)S(1)}, u32[]{:S(2)}, u32[]{:S(2)}) collective-permute-start(bf16[224,256]{1,0:T(8,128)(2,1)S(1)} %collective-permute-done.13), channel_id=1, source_target_pairs={{0,1},{1,2},{2,3},{3,4},{4,5},{5,6},{6,7},{7,8},{8,9},{9,10},{10,1... | collective-permute-start | bytes 344072 | tf_op jit(solution)/shard_map/ppermute | solution.py:136
  87.1 29.6 %copy-start.3 = (bf16[2,2,64,256]{3,2,1,0:T(8,128)(2,1)}, bf16[2,2,64,256]{3,2,1,0:T(8,128)(2,1)S(1)}, u32[]{:S(2)}) copy-start(bf16[2,2,64,256]{3,2,1,0:T(8,128)(2,1)S(1)} %get-tuple-element.204) | copy-start | bytes 393220
  87.4 24.0 %collective-permute-start.17 = (bf16[2,64,256]{2,1,0:T(8,128)(2,1)S(1)}, bf16[2,64,256]{2,1,0:T(8,128)(2,1)S(1)}, u32[]{:S(2)}, u32[]{:S(2)}) collective-permute-start(bf16[2,64,256]{2,1,0:T(8,128)(2,1)S(1)} %get-tuple-element.197), channel_id=1, source_target_pairs={{0,32},{32,0},{1,33},{33,1},{2,34},{34,2},{3,35},{35,3},{4,36},{36... | collective-permute-start | bytes 196616 | tf_op jit(solution)/shard_map/ppermute | solution.py:93
  111.5 8.7 %collective-permute-start.18 = (bf16[2,2,64,256]{3,2,1,0:T(8,128)(2,1)S(1)}, bf16[2,2,64,256]{3,2,1,0:T(8,128)(2,1)S(1)}, u32[]{:S(2)}, u32[]{:S(2)}) collective-permute-start(bf16[2,2,64,256]{3,2,1,0:T(8,128)(2,1)S(1)} %get-tuple-element.195), channel_id=1, source_target_pairs={{0,256},{256,512},{512,768},{768,0},{1,257},{257,513},{513,769},{7... | collective-permute-start | bytes 393224 | tf_op jit(solution)/shard_map/ppermute | solution.py:100
  116.8 5.7 %collective-permute-start.20 = (bf16[2,2,64,256]{3,2,1,0:T(8,128)(2,1)S(1)}, bf16[2,2,64,256]{3,2,1,0:T(8,128)(2,1)S(1)}, u32[]{:S(2)}, u32[]{:S(2)}) collective-permute-start(bf16[2,2,64,256]{3,2,1,0:T(8,128)(2,1)S(1)} %get-tuple-element.195), channel_id=1, source_target_pairs={{0,768},{256,0},{512,256},{768,512},{1,769},{257,1},{513,257},{769... | collective-permute-start | bytes 393224 | tf_op jit(solution)/shard_map/ppermute | solution.py:101
  120.2 6.9 %collective-permute-start.19 = (bf16[2,2,64,256]{3,2,1,0:T(8,128)(2,1)S(1)}, bf16[2,2,64,256]{3,2,1,0:T(8,128)(2,1)S(1)}, u32[]{:S(2)}, u32[]{:S(2)}) collective-permute-start(bf16[2,2,64,256]{3,2,1,0:T(8,128)(2,1)S(1)} %collective-permute-done.18), channel_id=1, source_target_pairs={{0,256},{256,512},{512,768},{768,0},{1,257},{257,513},{513,769},{7... | collective-permute-start | bytes 393224 | tf_op jit(solution)/shard_map/ppermute | solution.py:102
  127.2 11.2 %collective-permute-start.21 = (bf16[4,2,2,64,256]{4,3,2,1,0:T(8,128)(2,1)S(1)}, bf16[4,2,2,64,256]{4,3,2,1,0:T(8,128)(2,1)S(1)}, u32[]{:S(2)}, u32[]{:S(2)}) collective-permute-start(bf16[4,2,2,64,256]{4,3,2,1,0:T(8,128)(2,1)S(1)} %get-tuple-element.181), channel_id=1, source_target_pairs={{0,64},{64,128},{128,192},{192,0},{1,65},{65,129},{129,193},{193,1... | collective-permute-start | bytes 1572872 | tf_op jit(solution)/shard_map/ppermute | solution.py:100
  130.8 11.3 %collective-permute-start.23 = (bf16[4,2,2,64,256]{4,3,2,1,0:T(8,128)(2,1)S(1)}, bf16[4,2,2,64,256]{4,3,2,1,0:T(8,128)(2,1)S(1)}, u32[]{:S(2)}, u32[]{:S(2)}) collective-permute-start(bf16[4,2,2,64,256]{4,3,2,1,0:T(8,128)(2,1)S(1)} %get-tuple-element.181), channel_id=1, source_target_pairs={{0,192},{64,0},{128,64},{192,128},{1,193},{65,1},{129,65},{193,129... | collective-permute-start | bytes 1572872 | tf_op jit(solution)/shard_map/ppermute | solution.py:101
  138.4 16.4 %collective-permute-start.22 = (bf16[4,2,2,64,256]{4,3,2,1,0:T(8,128)(2,1)S(1)}, bf16[4,2,2,64,256]{4,3,2,1,0:T(8,128)(2,1)S(1)}, u32[]{:S(2)}, u32[]{:S(2)}) collective-permute-start(bf16[4,2,2,64,256]{4,3,2,1,0:T(8,128)(2,1)S(1)} %collective-permute-done.21), channel_id=1, source_target_pairs={{0,64},{64,128},{128,192},{192,0},{1,65},{65,129},{129,193},{193,1... | collective-permute-start | bytes 1572872 | tf_op jit(solution)/shard_map/ppermute | solution.py:102
  201.3 16.2 %collective-permute-start.24 = (bf16[2,64,896]{2,1,0:T(8,128)(2,1)S(1)}, bf16[2,64,896]{2,1,0:T(8,128)(2,1)S(1)}, u32[]{:S(2)}, u32[]{:S(2)}) collective-permute-start(bf16[2,64,896]{2,1,0:T(8,128)(2,1)S(1)} %squeeze.39), channel_id=1, source_target_pairs={{0,16},{16,0},{1,17},{17,1},{2,18},{18,2},{3,19},{19,3},{4,20},{20... | collective-permute-start | bytes 688136 | tf_op jit(solution)/shard_map/ppermute | solution.py:93
